TPU v7x, 32 devices: a whole 2x2x4 slice. The times are simulated.
32 devices in a mesh: group: 2 (over y), seq: 8 (over z, x), chan: 2 (over core).
Axes of the slice: x: 2, y: 2, z: 4, core: 2. Of those that a mesh axis runs over, the one named last changes fastest.
Arguments:
- fresh: bfloat16 [2048, 3, 2048], P(('group', 'seq'), None, 'chan'), parts along dimension 0, may hold values from -6 to 6
- library: bfloat16 [8, 8, 2048], P('seq', None, 'chan'), may hold values from -6 to 6
- block_slot: int32 [8], replicated, may hold values from 0 to 7, each once
- prefix_blocks: int32 [16, 4], P('group'), parts along dimension 0, may hold values from 0 to 7, all different within a row
- short_taps: float32 [3, 3, 2048], P(None, None, 'chan'), may hold values from -4 to 4
- long_filter: float32 [1024, 2048], P('seq', 'chan'), may hold values from -2 to 2
- skip_gain: float32 [2048], P('chan'), may hold values from -6 to 6
Outputs:
- mixed: bfloat16 [2048, 2048], P(('group', 'seq'), 'chan'), parts along dimension 0
There are 2 independent parts, one for each index of `group`. A program takes and returns all parts, laid end to end along the dimension named above; an argument that names none is the same for every part. Nothing has to cross between parts.
Inputs may be any that keep to these rules, and one draw needn't show every extreme that they name: `block_slot`: each number appears once. `prefix_blocks`: every library block is named at least once; the four entries of a row differ.
All inputs are finite; a program needn't handle non-finite values.
Results may differ from a plain program's by a relative error of at most 0.008.
Values may be sent and summed in bfloat16 or wider, within the bound.
No kernel may reach another device: no remote copies, remote signals or barrier semaphores. Data moves between devices by JAX's collectives and lax.ppermute only.
A program may use at most 64 MiB of HBM per device.

v0:
```python
import math
import jax
import jax.numpy as jnp
from jax import lax
from jax.sharding import PartitionSpec as P

TAPS = 3
BLK = 8


def from_behind(shard, axis, by):
    count = lax.axis_size(axis)
    pairs = [(i, i + by) for i in range(count) if 0 <= i + by < count]
    return lax.ppermute(shard, axis, pairs)


def exact_dot(pattern, matrix, tensor):
    return jnp.einsum(pattern, matrix, tensor, precision=lax.Precision.HIGHEST)


def turn_angles(numbers, period):
    return (numbers % period).astype(jnp.float32) * (2.0 * math.pi / period)


def ring_body(fresh, library, block_slot, prefix_blocks, short_taps, long_filter, skip_gain):
    row_count = fresh.shape[0]
    channels = fresh.shape[2]
    devices = lax.axis_size("seq")
    seq_index = lax.axis_index("seq")
    group_rows = row_count // devices
    period = 2 * row_count * devices
    block_ids = jnp.arange(devices, dtype=jnp.int32)
    mode_ids = jnp.arange(2 * devices, dtype=jnp.int32)
    coarse = turn_angles(mode_ids[:, None] * block_ids[None, :], 2 * devices)
    cos_q = jnp.cos(coarse)
    sin_q = jnp.sin(coarse)
    local_rows = seq_index * group_rows + jnp.arange(group_rows, dtype=jnp.int32)
    twist = turn_angles(mode_ids[:, None] * local_rows[None, :], period)
    twist_cos = jnp.cos(twist)[:, :, None]
    twist_sin = jnp.sin(twist)[:, :, None]
    row_ids = jnp.arange(row_count, dtype=jnp.int32)
    fine_angles = turn_angles(row_ids[:, None] * row_ids[None, :], row_count)
    cos_m = jnp.cos(fine_angles)
    sin_m = jnp.sin(fine_angles)
    first_modes = 2 * seq_index + jnp.arange(2, dtype=jnp.int32)
    back_twist = turn_angles(first_modes[:, None] * row_ids[None, :], period)
    back_cos = jnp.cos(back_twist)[:, :, None]
    back_sin = jnp.sin(back_twist)[:, :, None]

    def to_modes(column):
        real_part = exact_dot("kq,qgc->kgc", cos_q, column)
        imag_part = -exact_dot("kq,qgc->kgc", sin_q, column)
        return jnp.stack(
            [
                real_part * twist_cos + imag_part * twist_sin,
                imag_part * twist_cos - real_part * twist_sin,
            ]
        )

    def to_spectrum(spread):
        real_part = exact_dot("ki,jic->jkc", cos_m, spread[0]) + exact_dot(
            "ki,jic->jkc", sin_m, spread[1]
        )
        imag_part = exact_dot("ki,jic->jkc", cos_m, spread[1]) - exact_dot(
            "ki,jic->jkc", sin_m, spread[0]
        )
        return (real_part, imag_part)

    blocks_here = row_count // BLK
    flat_ids = prefix_blocks.reshape(-1)
    first_block = jnp.minimum(seq_index * blocks_here, flat_ids.shape[0] - blocks_here)
    own_ids = lax.dynamic_slice_in_dim(flat_ids, first_block, blocks_here)
    matches = own_ids[:, None] == jnp.arange(block_slot.shape[0], dtype=jnp.int32)[None, :]
    wanted = jnp.sum(jnp.where(matches, block_slot[None, :], 0), axis=1)
    shards = lax.all_gather(library, "seq", axis=0, tiled=True)
    picker = (wanted[:, None] == jnp.arange(shards.shape[0], dtype=jnp.int32)[None, :]).astype(
        jnp.bfloat16
    )
    gathered = jnp.einsum("bn,nlc->blc", picker, shards, preferred_element_type=jnp.float32)
    cached = gathered.reshape(row_count, channels).astype(jnp.bfloat16)
    values = jnp.where(seq_index < devices // 4, cached, fresh[:, 2])
    stacked = jnp.concatenate([fresh[:, :2], values[:, None]], axis=1)
    previous = from_behind(stacked[row_count - (TAPS - 1) :], "seq", 1)
    extended = jnp.concatenate([previous, stacked], axis=0)
    shortened = jnp.zeros((row_count, 3, channels), jnp.float32)
    for offset in range(TAPS):
        window_start = TAPS - 1 - offset
        shortened = shortened + short_taps[offset][None] * extended[
            window_start : window_start + row_count
        ].astype(jnp.float32)
    gating = shortened[:, 0]
    signal = shortened[:, 1] * shortened[:, 2]
    spread_signal = to_modes(
        lax.all_to_all(signal[None], "seq", split_axis=1, concat_axis=0, tiled=True)
    )
    spread_taps = to_modes(
        lax.all_to_all(long_filter[None], "seq", split_axis=1, concat_axis=0, tiled=True)
    )
    moved_signal, moved_taps = (
        lax.all_to_all(
            spread_signal.astype(jnp.bfloat16), "seq", split_axis=1, concat_axis=2, tiled=True
        ).astype(spread_signal.dtype),
        lax.all_to_all(
            spread_taps.astype(jnp.bfloat16), "seq", split_axis=1, concat_axis=2, tiled=True
        ).astype(spread_taps.dtype),
    )
    sig_real, sig_imag = to_spectrum(moved_signal)
    tap_real, tap_imag = to_spectrum(moved_taps)
    prod_real = sig_real * tap_real - sig_imag * tap_imag
    prod_imag = sig_real * tap_imag + sig_imag * tap_real
    back_real = exact_dot("ki,jic->jkc", cos_m, prod_real) - exact_dot(
        "ki,jic->jkc", sin_m, prod_imag
    )
    back_imag = exact_dot("ki,jic->jkc", cos_m, prod_imag) + exact_dot(
        "ki,jic->jkc", sin_m, prod_real
    )
    turned = jnp.stack(
        [back_real * back_cos - back_imag * back_sin, back_imag * back_cos + back_real * back_sin]
    )
    spread = lax.all_to_all(turned, "seq", split_axis=2, concat_axis=1, tiled=True)
    positions = (
        exact_dot("kq,kgc->qgc", cos_q, spread[0]) - exact_dot("kq,kgc->qgc", sin_q, spread[1])
    ) / period
    convolved = lax.all_to_all(positions, "seq", split_axis=0, concat_axis=1, tiled=True)[0]
    output = gating * (convolved + skip_gain[None, :] * signal)
    return output.astype(jnp.bfloat16)


def dft_tables(tokens):
    period = 2 * tokens
    width = 1
    while width * width < tokens:
        width *= 2
    outer = tokens // width
    freqs = jnp.arange(tokens + 1, dtype=jnp.int32)[:, None]
    coarse = turn_angles(freqs * (width * jnp.arange(outer, dtype=jnp.int32))[None, :], period)
    fine = turn_angles(freqs * jnp.arange(width, dtype=jnp.int32)[None, :], period)
    c1, s1 = (jnp.cos(coarse)[:, :, None], jnp.sin(coarse)[:, :, None])
    c2, s2 = (jnp.cos(fine)[:, None, :], jnp.sin(fine)[:, None, :])
    cos_t = (c1 * c2 - s1 * s2).reshape(tokens + 1, tokens)
    sin_t = (s1 * c2 + c1 * s2).reshape(tokens + 1, tokens)
    return (cos_t, sin_t)


def local_body(fresh, library, block_slot, prefix_blocks, short_taps, long_filter, skip_gain):
    row_count, _, channels = fresh.shape
    devices = lax.axis_size("seq")
    seq_index = lax.axis_index("seq")
    tokens = row_count * devices
    own = channels // devices
    lib_here = library.shape[0]
    lib_rows = lib_here * BLK // 4
    packed = jnp.concatenate([fresh, long_filter.astype(jnp.bfloat16)[:, None, :]], axis=1)
    packed = jnp.concatenate([packed, library.reshape(lib_rows, 4, channels)], axis=0)
    moved = lax.all_to_all(packed, "seq", split_axis=2, concat_axis=0, tiled=True)
    moved = moved.reshape(devices, row_count + lib_rows, 4, own)
    rows = moved[:, :row_count].reshape(tokens, 4, own)
    lib_all = moved[:, row_count:].reshape(devices * lib_here, BLK * own)
    slot_ids = block_slot[prefix_blocks.reshape(-1)]
    prefix_len = slot_ids.shape[0] * BLK
    picker = (slot_ids[:, None] == jnp.arange(lib_all.shape[0], dtype=jnp.int32)[None, :]).astype(
        jnp.bfloat16
    )
    cached = jnp.dot(picker, lib_all, preferred_element_type=jnp.float32)
    cached = cached.reshape(prefix_len, own).astype(jnp.bfloat16)
    values = jnp.concatenate([cached, rows[prefix_len:, 2]], axis=0)
    stacked = jnp.concatenate([rows[:, :2], values[:, None]], axis=1).astype(jnp.float32)
    taps = lax.dynamic_slice_in_dim(short_taps, seq_index * own, own, axis=2)
    gain = lax.dynamic_slice_in_dim(skip_gain, seq_index * own, own, axis=0)
    shortened = jnp.zeros((tokens, 3, own), jnp.float32)
    for offset in range(TAPS):
        shifted = jnp.pad(stacked[: tokens - offset], ((offset, 0), (0, 0), (0, 0)))
        shortened = shortened + taps[offset][None] * shifted
    gating = shortened[:, 0]
    signal = shortened[:, 1] * shortened[:, 2]
    cos_t, sin_t = dft_tables(tokens)
    table = jnp.concatenate([cos_t, sin_t], axis=0).astype(jnp.bfloat16)
    operands = jnp.concatenate([signal.astype(jnp.bfloat16), rows[:, 3]], axis=1)
    spec = jnp.dot(table, operands, preferred_element_type=jnp.float32)
    bins = tokens + 1
    sig_c, tap_c = (spec[:bins, :own], spec[:bins, own:])
    sig_s, tap_s = (spec[bins:, :own], spec[bins:, own:])
    weight = jnp.where((jnp.arange(bins) == 0) | (jnp.arange(bins) == tokens), 1.0, 2.0).astype(
        jnp.float32
    )[:, None] / (2 * tokens)
    real = (sig_c * tap_c - sig_s * tap_s) * weight
    turned = (sig_c * tap_s + sig_s * tap_c) * weight
    back = jnp.concatenate([real, turned], axis=0).astype(jnp.bfloat16)
    convolved = lax.dot_general(
        table, back, (((0,), (0,)), ((), ())), preferred_element_type=jnp.float32
    )
    output = (gating * (convolved + gain[None, :] * signal)).astype(jnp.bfloat16)
    return lax.all_to_all(output, "seq", split_axis=0, concat_axis=1, tiled=True)


def body(fresh, library, *rest):
    devices = lax.axis_size("seq")
    tokens = fresh.shape[0] * devices
    fits = tokens <= 4096 and fresh.shape[2] % devices == 0 and (library.shape[0] * BLK % 4 == 0)
    if fits:
        return local_body(fresh, library, *rest)
    return ring_body(fresh, library, *rest)


def solution(mesh):
    return jax.shard_map(
        body,
        mesh=mesh,
        in_specs=(
            P(("group", "seq"), None, "chan"),
            P("seq", None, "chan"),
            P(),
            P("group", None),
            P(None, None, "chan"),
            P("seq", "chan"),
            P("chan"),
        ),
        out_specs=P(("group", "seq"), "chan"),
        check_vma=False,
    )
```

profile of v0, /device:TPU:0, one launch (start us, length us, event | category | flops | bytes accessed | tf_op | source)
XLA Modules:
  0.0 86.8 jit_solution(6593084510004803457)
XLA Ops:
  0.0 0.0 copy-start
  0.0 0.0 copy-start.3
  0.0 0.8 reshape.169
  0.8 1.1 %convert_bitcast_fusion = bf16[128,1,1024]{2,0,1:T(8,128)(2,1)S(1)} fusion(f32[128,1024]{1,0:T(8,128)} %param.12), kind=kLoop, calls=%fused_computation.27 | loop fusion | flops 131072 | bytes 786432 | tf_op jit(solution)/shard_map/broadcast_in_dim | solution.py:153
  1.9 0.4 copy.37
  2.3 0.7 copy.38
  3.1 0.0 copy-done.3
  3.1 0.7 copy.36
  3.8 2.9 %pad_maximum_fusion.3 = bf16[130,4,1024]{0,1,2:T(4,128)(2,1)} fusion(bf16[2,4,1024]{0,1,2:T(4,128)(2,1)S(1)} %copy.38, bf16[128,1,1024]{0,1,2:T(2,128)(2,1)S(1)} %copy.37, bf16[128,3,1024]{0,1,2:T(4,128)(2,1)S(1)} %copy.36), kind=kLoop, calls=%fused_computation.6 | loop fusion | flops 3194880 | bytes 2129920 | tf_op jit(solution)/shard_map/concatenate | solution.py:154
  6.7 0.0 copy-start.4
  6.7 7.4 %all-to-all-start = ((bf16[130,4,1024]{0,1,2:T(4,128)(2,1)}), bf16[130,4,1024]{0,1,2:T(4,128)(2,1)S(1)}, u32[]{:S(2)}, u32[]{:S(2)}) async-start(bf16[130,4,1024]{0,1,2:T(4,128)(2,1)} %pad_maximum_fusion.3), calls=%async_computation | async-start | bytes 4194304 | tf_op jit(solution)/shard_map/all_to_all | solution.py:155
  14.1 0.0 copy-done.4
  14.1 0.1 copy.41
  14.2 0.1 reshape.171
  14.3 0.8 dynamic_slice.7
  15.0 0.0 copy-done
  15.0 0.7 gather_fusion
  15.7 0.7 dynamic-slice_bitcast_fusion.2
  16.5 0.6 fusion.25
  17.1 0.7 fusion.28
  17.7 3.7 %subtract_convert_fusion = (bf16[1025,32,32]{0,2,1:T(8,128)(2,1)}, bf16[1025,32,32]{0,2,1:T(8,128)(2,1)}) fusion(f32[1025,32]{0,1:T(8,128)S(1)} %get-tuple-element.14, f32[1025,32]{0,1:T(8,128)S(1)} %get-tuple-element.13, f32[1025,32]{0,1:T(8,128)S(1)} %get-tuple-element.15, f32[1025,32]{0,1:T(8,128)S(1)} %get-tuple-element.12), kind=kLoop, calls=%fused_computation.2 | loop fusion | flops 8396800 | bytes 4723200 | tf_op jit(solution)/shard_map/convert.5
  21.4 40.9 %all-to-all-done = bf16[130,4,1024]{0,1,2:T(4,128)(2,1)S(1)} async-done(((bf16[130,4,1024]{0,1,2:T(4,128)(2,1)}), bf16[130,4,1024]{0,1,2:T(4,128)(2,1)S(1)}, u32[]{:S(2)}, u32[]{:S(2)}) %all-to-all-start) | async-done | bytes 1064992 | tf_op jit(solution)/shard_map/all_to_all | solution.py:155
  62.3 3.9 %copy.43 = bf16[130,4,8,128]{3,2,1,0:T(8,128)(2,1)S(1)} copy(bf16[130,4,8,128]{0,1,3,2:T(4,128)(2,1)S(1)} %bitcast.44) | data formatting | bytes 2129920 | tf_op jit(solution)/shard_map/all_to_all | solution.py:155
  66.3 0.1 slice.70
  66.3 0.4 copy.40
  66.8 0.2 convolution_convert_fusion
  67.1 0.1 maximum_convert_fusion
  67.2 0.0 copy-start.1
  67.2 0.0 copy-start.2
  67.2 0.5 multiply_add_fusion
  67.8 0.1 fusion.12
  67.9 1.0 %copy-done.1 = bf16[1025,32,32]{0,2,1:T(8,128)(2,1)S(1)} copy-done((bf16[1025,32,32]{0,2,1:T(8,128)(2,1)S(1)}, bf16[1025,32,32]{0,2,1:T(8,128)(2,1)}, u32[]{:S(2)}) %copy-start.1) | copy-done | bytes 2099224
  68.9 0.7 copy-done.2
  69.6 2.2 %fusion.1 = f32[2050,256]{1,0:T(8,128)S(1)} fusion(bf16[1025,1024]{0,1:T(8,128)(2,1)S(1)} %bitcast.52, bf16[1025,1024]{0,1:T(8,128)(2,1)S(1)} %bitcast.50, bf16[1024,128]{1,0:T(8,128)(2,1)S(1)} %slice_bitcast_fusion.1, bf16[1024,128]{1,0:T(8,128)(2,1)S(1)} %fusion.12), kind=kOutput, calls=%fused_computation.5 | convolution fusion | flops 1084235776 | bytes 6821888 | tf_op jit(solution)/shard_map/dot_general | solution.py:179
  71.8 0.3 multiply_convert_fusion.1
  72.1 1.4 %fusion.4 = bf16[1024,128]{1,0:T(8,128)(2,1)S(1)} fusion(bf16[1025,1024]{0,1:T(8,128)(2,1)S(1)} %bitcast.53, bf16[1025,1024]{0,1:T(8,128)(2,1)S(1)} %bitcast.51, bf16[1025,128]{1,0:T(8,128)(2,1)S(1)} %get-tuple-element.6, bf16[1025,128]{1,0:T(8,128)(2,1)S(1)} %get-tuple-element.5, f32[1024,3,128]{2,0,1:T(8,128)S(1)} %multiply_add_fusion, ...), kind=kOutput, calls=%fused_computation.10 | convolution fusion | flops 547496960 | bytes 6558720 | tf_op jit(solution)/shard_map/dot_general | solution.py:189
  73.5 12.5 %all_to_all.34 = bf16[8,128,128]{2,1,0:T(8,128)(2,1)S(1)} all-to-all(bf16[8,128,128]{2,1,0:T(8,128)(2,1)S(1)} %bitcast.54), channel_id=1, replica_groups=mesh['group'=2,'seq'=8,'chan'=2] {'seq'}, dimensions={0} | all-to-all | bytes 524288 | tf_op jit(solution)/shard_map/all_to_all | solution.py:193
  86.0 0.7 copy_bitcast_fusion
  (10 shorter events, 0.1 us)
Async XLA Ops:
  0.0 15.0 %copy-start = (s32[8]{0:T(128)S(1)}, s32[8]{0:T(128)}, u32[]{:S(2)}) copy-start(s32[8]{0:T(128)} %param.9) | copy-start | bytes 100
  0.0 3.1 %copy-start.3 = (bf16[128,3,1024]{2,0,1:T(8,128)(2,1)S(1)}, bf16[128,3,1024]{2,0,1:T(8,128)(2,1)}, u32[]{:S(2)}) copy-start(bf16[128,3,1024]{2,0,1:T(8,128)(2,1)} %param.7) | copy-start | bytes 2359300
  6.7 7.4 %copy-start.4 = (s32[8,4]{0,1:T(4,128)S(1)}, s32[8,4]{0,1:T(4,128)}, u32[]{:S(2)}) copy-start(s32[8,4]{0,1:T(4,128)} %param.10) | copy-start | bytes 388
  6.7 55.7 %all-to-all-start = ((bf16[130,4,1024]{0,1,2:T(4,128)(2,1)}), bf16[130,4,1024]{0,1,2:T(4,128)(2,1)S(1)}, u32[]{:S(2)}, u32[]{:S(2)}) async-start(bf16[130,4,1024]{0,1,2:T(4,128)(2,1)} %pad_maximum_fusion.3), calls=%async_computation | async-start | bytes 4194304 | tf_op jit(solution)/shard_map/all_to_all | solution.py:155
  67.2 1.7 %copy-start.1 = (bf16[1025,32,32]{0,2,1:T(8,128)(2,1)S(1)}, bf16[1025,32,32]{0,2,1:T(8,128)(2,1)}, u32[]{:S(2)}) copy-start(bf16[1025,32,32]{0,2,1:T(8,128)(2,1)} %get-tuple-element.7) | copy-start | bytes 6297604
  67.2 2.4 %copy-start.2 = (bf16[1025,32,32]{0,2,1:T(8,128)(2,1)S(1)}, bf16[1025,32,32]{0,2,1:T(8,128)(2,1)}, u32[]{:S(2)}) copy-start(bf16[1025,32,32]{0,2,1:T(8,128)(2,1)} %get-tuple-element.8) | copy-start | bytes 6297604
where the time goes:
time: 87.2 us; the launch traced here: 86.8 us
  waiting for transfers between devices  40.9 us (47%)
  blocking collectives  12.5 us (14%)
  local copies, waits for them, and re-layouts  12 us (14%)
  other arithmetic  9.91 us (11%)
  starting transfers between devices  7.41 us (8%)
  matrix products  3.8 us (4%)
    all_to_all x1, waiting for transfers between devices, local_body(): lax.all_to_all(packed, 'seq', split_axis=2, concat_axis=0, tiled=True)  40.9 us
    all_to_all x1, blocking collectives, local_body(): lax.all_to_all(output, 'seq', split_axis=0, concat_axis=1, tiled=True)  12.5 us
    all_to_all x1, starting transfers between devices, local_body(): lax.all_to_all(packed, 'seq', split_axis=2, concat_axis=0, tiled=True)  7.41 us
    another operation x2, other arithmetic  3.99 us
    all_to_all x1, local copies, waits for them, and re-layouts, local_body(): lax.all_to_all(packed, 'seq', split_axis=2, concat_axis=0, tiled=True)  3.92 us
    concatenate x1, other arithmetic, local_body(): jnp.concatenate([packed, library.reshape(lib_rows, 4, channels)], axis=0)  2.86 us
    unnamed x12, local copies, waits for them, and re-layouts  2.58 us
    dot_general x1, matrix products, local_body(): spec = jnp.dot(table, operands, preferred_element_type=jnp.float32)  2.2 us
  transfers between devices with their start and end apart: 1, of which 1 were waited for; matrix products, arithmetic and copies ran while one was open for 8% of the time, Pallas kernels for 0%

commit v1 on v0

--- a/solution.py
+++ b/solution.py
@@ -6,6 +6,18 @@
 
 TAPS = 3
 BLK = 8
+
+
+def get_waves_for(w_in, axis_id):
+    return jnp.concatenate(
+        jax.lax.all_to_all(
+            jnp.stack(jnp.split(w_in, jax.lax.axis_size(axis_id), 2), 0),
+            axis_id,
+            split_axis=0,
+            concat_axis=0,
+        ),
+        0,
+    )
 
 
 def from_behind(shard, axis, by):
@@ -152,7 +164,7 @@
     lib_rows = lib_here * BLK // 4
     packed = jnp.concatenate([fresh, long_filter.astype(jnp.bfloat16)[:, None, :]], axis=1)
     packed = jnp.concatenate([packed, library.reshape(lib_rows, 4, channels)], axis=0)
-    moved = lax.all_to_all(packed, "seq", split_axis=2, concat_axis=0, tiled=True)
+    moved = get_waves_for(packed, axis_id="seq")
     moved = moved.reshape(devices, row_count + lib_rows, 4, own)
     rows = moved[:, :row_count].reshape(tokens, 4, own)
     lib_all = moved[:, row_count:].reshape(devices * lib_here, BLK * own)

time: 87.2 us -> 59.6 us (0.68)
  waiting for transfers between devices: 40.9 us -> 18.8 us
  local copies, waits for them, and re-layouts: 12 us -> 8.2 us
  other arithmetic: 9.91 us -> 8.27 us
    all_to_all x1, waiting for transfers between devices: 40.9 us -> 18.8 us  [get_waves_for(): jax.lax.all_to_all(jnp.stack(jnp.split(w_in, jax.lax.axis_size(axis_id),...]
    all_to_all x1 -> x0, local copies, waits for them, and re-layouts: 3.92 us -> none  [local_body(): lax.all_to_all(packed, 'seq', split_axis=2, concat_axis=0, tiled=True)]
    concatenate x1, other arithmetic: 2.86 us -> 1.25 us  [local_body(): jnp.concatenate([packed, library.reshape(lib_rows, 4, channels)], axis=0)]
    another operation x0 -> x2, local copies, waits for them, and re-layouts: none -> 1.48 us  [get_waves_for(): jnp.stack(jnp.split(w_in, jax.lax.axis_size(axis_id), 2), 0)]
    unnamed x12 -> x17, local copies, waits for them, and re-layouts: 2.58 us -> 2.24 us
  transfers between devices with their start and end apart: 1 -> 1, of which waited for: 1 -> 1; matrix products, arithmetic and copies ran while one was open for 8% -> 12% of each run, Pallas kernels for 0% -> 0%
where the time goes in v1:
time: 59.6 us; the launch traced here: 59.2 us
  waiting for transfers between devices  18.8 us (32%)
  blocking collectives  12.5 us (21%)
  other arithmetic  8.27 us (14%)
  local copies, waits for them, and re-layouts  8.2 us (14%)
  starting transfers between devices  7.41 us (12%)
  matrix products  3.79 us (6%)
    all_to_all x1, waiting for transfers between devices, get_waves_for(): jax.lax.all_to_all(jnp.stack(jnp.split(w_in, jax.lax.axis_size(axis_id),...  18.8 us
    all_to_all x1, blocking collectives, local_body(): lax.all_to_all(output, 'seq', split_axis=0, concat_axis=1, tiled=True)  12.5 us
    all_to_all x1, starting transfers between devices, get_waves_for(): jax.lax.all_to_all(jnp.stack(jnp.split(w_in, jax.lax.axis_size(axis_id),...  7.41 us
    another operation x2, other arithmetic  3.96 us
    unnamed x17, local copies, waits for them, and re-layouts  2.24 us
    dot_general x1, matrix products, local_body(): spec = jnp.dot(table, operands, preferred_element_type=jnp.float32)  2.19 us
    another operation x2, local copies, waits for them, and re-layouts, get_waves_for(): jnp.stack(jnp.split(w_in, jax.lax.axis_size(axis_id), 2), 0)  1.48 us
    dot_general x1, matrix products, local_body(): lax.dot_general(table, back, (((0,), (0,)), ((), ())), preferred_element_...  1.39 us
  transfers between devices with their start and end apart: 1, of which 1 were waited for; matrix products, arithmetic and copies ran while one was open for 12% of the time, Pallas kernels for 0%

profile of v1, /device:TPU:0, one launch (start us, length us, event | category | flops | bytes accessed | tf_op | source)
XLA Modules:
  0.0 59.2 jit_solution(14912400624332706978)
XLA Ops:
  0.0 0.0 copy-start
  0.0 0.7 %reshape.167 = bf16[2,4,1024]{2,1,0:T(4,128)(2,1)S(1)} reshape(bf16[1,8,1024]{2,1,0:T(8,128)(2,1)} %param.8) | data formatting | bytes 32768 | tf_op jit(solution)/shard_map/reshape | solution.py:166
  0.8 1.1 %convert_bitcast_fusion = bf16[128,1,1024]{2,0,1:T(8,128)(2,1)S(1)} fusion(f32[128,1024]{1,0:T(8,128)} %param.12), kind=kLoop, calls=%fused_computation.27 | loop fusion | flops 131072 | bytes 786432 | tf_op jit(solution)/shard_map/broadcast_in_dim | solution.py:165
  1.8 1.2 %pad_maximum_fusion.9 = bf16[130,4,1024]{2,0,1:T(8,128)(2,1)S(1)} fusion(bf16[2,4,1024]{2,0,1:T(2,128)(2,1)S(1)} %copy.32, bf16[128,1,1024]{2,0,1:T(8,128)(2,1)S(1)} %convert_bitcast_fusion, bf16[128,3,1024]{2,0,1:T(8,128)(2,1)} %param.7), kind=kLoop, calls=%fused_computation.11 | loop fusion | flops 3194880 | bytes 2129920 | tf_op jit(solution)/shard_map/concatenate | solution.py:166
  3.1 0.1 fusion.31
  3.2 0.1 fusion.30
  3.3 0.1 fusion.29
  3.3 0.1 fusion.28
  3.4 0.1 fusion.27
  3.4 0.1 fusion.26
  3.5 0.1 fusion.25
  3.6 1.4 %copy.33 = bf16[8,130,4,128]{3,2,1,0:T(4,128)(2,1)} copy(bf16[8,130,4,128]{3,1,2,0:T(8,128)(2,1)S(1)} %fusion.25) | data formatting | bytes 2129920 | tf_op jit(solution)/shard_map/stack | solution.py:14
  5.0 0.0 copy-start.3
  5.0 7.4 %all-to-all-start = ((bf16[8,130,4,128]{3,2,1,0:T(4,128)(2,1)}), bf16[8,130,4,128]{3,2,1,0:T(4,128)(2,1)S(1)}, u32[]{:S(2)}, u32[]{:S(2)}) async-start(bf16[8,130,4,128]{3,2,1,0:T(4,128)(2,1)} %copy.33), calls=%async_computation | async-start | bytes 2129920 | tf_op jit(solution)/shard_map/all_to_all | solution.py:13
  12.4 0.0 copy-done.3
  12.4 0.1 copy.35
  12.5 0.1 reshape.169
  12.6 0.8 %dynamic_slice.7 = f32[128]{0:T(128)S(1)} dynamic-slice(f32[1024]{0:T(1024)} %param.13, s32[]{:T(128)S(6)} %select_n.53), dynamic_slice_sizes={128} | dynamic-slice | bytes 1028 | tf_op jit(solution)/shard_map/dynamic_slice | solution.py:181
  13.3 0.0 copy-done
  13.4 0.7 %gather_fusion = s32[32]{0:T(128)S(1)} fusion(s32[8]{0:T(128)S(1)} %copy-done, s32[1024]{0:T(1024)S(1)} %pad_clamp_fusion), kind=kCustom, calls=%fused_computation | custom fusion | bytes 384 | tf_op jit(solution)/shard_map/gather | solution.py:171
  14.1 0.7 %dynamic-slice_bitcast_fusion.2 = (f32[3,128]{1,0:T(4,128)S(1)}, f32[3,128]{1,0:T(4,128)S(1)}, f32[3,128]{1,0:T(4,128)S(1)}) fusion(f32[3,3,1024]{2,1,0:T(4,128)} %param.11, s32[]{:T(128)S(6)} %select_n.53, s32[]{:T(128)S(6)} %add.79, s32[]{:T(128)S(6)} %add.80), kind=kLoop, calls=%fused_computation.78 | loop fusion | bytes 9228 | tf_op jit(solution)/shard_map/mul | solution.py:185
  14.8 0.6 fusion.33
  15.4 0.7 %fusion.36 = (f32[1025,32]{0,1:T(8,128)S(1)}, f32[1025,32]{0,1:T(8,128)S(1)}) fusion(s32[32]{0:T(128)S(1)} %iota_multiply_fusion), kind=kLoop, calls=%fused_computation.67 | loop fusion | flops 459200 | bytes 262528 | tf_op jit(solution)/shard_map/cos | solution.py:150
  16.0 3.7 %subtract_convert_fusion = (bf16[1025,32,32]{0,2,1:T(8,128)(2,1)}, bf16[1025,32,32]{0,2,1:T(8,128)(2,1)}) fusion(f32[1025,32]{0,1:T(8,128)S(1)} %get-tuple-element.14, f32[1025,32]{0,1:T(8,128)S(1)} %get-tuple-element.13, f32[1025,32]{0,1:T(8,128)S(1)} %get-tuple-element.15, f32[1025,32]{0,1:T(8,128)S(1)} %get-tuple-element.12), kind=kLoop, calls=%fused_computation.2 | loop fusion | flops 8396800 | bytes 4723200 | tf_op jit(solution)/shard_map/convert.5
  19.7 18.8 %all-to-all-done = bf16[8,130,4,128]{3,2,1,0:T(4,128)(2,1)S(1)} async-done(((bf16[8,130,4,128]{3,2,1,0:T(4,128)(2,1)}), bf16[8,130,4,128]{3,2,1,0:T(4,128)(2,1)S(1)}, u32[]{:S(2)}, u32[]{:S(2)}) %all-to-all-start) | async-done | bytes 1064992 | tf_op jit(solution)/shard_map/all_to_all | solution.py:13
  38.5 0.4 slice.70
  38.9 0.2 copy.34
  39.3 0.2 convolution_convert_fusion
  39.5 0.1 maximum_convert_fusion
  39.6 0.0 copy-start.1
  39.7 0.0 copy-start.2
  39.7 0.5 multiply_add_fusion
  40.2 0.1 fusion.12
  40.3 1.0 %copy-done.1 = bf16[1025,32,32]{0,2,1:T(8,128)(2,1)S(1)} copy-done((bf16[1025,32,32]{0,2,1:T(8,128)(2,1)S(1)}, bf16[1025,32,32]{0,2,1:T(8,128)(2,1)}, u32[]{:S(2)}) %copy-start.1) | copy-done | bytes 2099224
  41.3 0.7 %copy-done.2 = bf16[1025,32,32]{0,2,1:T(8,128)(2,1)S(1)} copy-done((bf16[1025,32,32]{0,2,1:T(8,128)(2,1)S(1)}, bf16[1025,32,32]{0,2,1:T(8,128)(2,1)}, u32[]{:S(2)}) %copy-start.2) | copy-done | bytes 2099224
  42.0 2.2 %fusion.1 = f32[2050,256]{1,0:T(8,128)S(1)} fusion(bf16[1025,1024]{0,1:T(8,128)(2,1)S(1)} %bitcast.79, bf16[1025,1024]{0,1:T(8,128)(2,1)S(1)} %bitcast.77, bf16[1024,128]{1,0:T(8,128)(2,1)S(1)} %slice_bitcast_fusion.1, bf16[1024,128]{1,0:T(8,128)(2,1)S(1)} %fusion.12), kind=kOutput, calls=%fused_computation.5 | convolution fusion | flops 1084235776 | bytes 6821888 | tf_op jit(solution)/shard_map/dot_general | solution.py:191
  44.2 0.3 multiply_convert_fusion.1
  44.5 1.4 %fusion.4 = bf16[1024,128]{1,0:T(8,128)(2,1)S(1)} fusion(bf16[1025,1024]{0,1:T(8,128)(2,1)S(1)} %bitcast.80, bf16[1025,1024]{0,1:T(8,128)(2,1)S(1)} %bitcast.78, bf16[1025,128]{1,0:T(8,128)(2,1)S(1)} %get-tuple-element.6, bf16[1025,128]{1,0:T(8,128)(2,1)S(1)} %get-tuple-element.5, f32[1024,3,128]{2,0,1:T(8,128)S(1)} %multiply_add_fusion, ...), kind=kOutput, calls=%fused_computation.9 | convolution fusion | flops 547496960 | bytes 6558720 | tf_op jit(solution)/shard_map/dot_general | solution.py:201
  45.9 12.5 %all_to_all.24 = bf16[8,128,128]{2,1,0:T(8,128)(2,1)S(1)} all-to-all(bf16[8,128,128]{2,1,0:T(8,128)(2,1)S(1)} %bitcast.81), channel_id=1, replica_groups=mesh['group'=2,'seq'=8,'chan'=2] {'seq'}, dimensions={0} | all-to-all | bytes 524288 | tf_op jit(solution)/shard_map/all_to_all | solution.py:205
  58.4 0.7 %copy_bitcast_fusion = bf16[128,1024]{1,0:T(8,128)(2,1)} fusion(bf16[8,128,128]{2,1,0:T(8,128)(2,1)S(1)} %all_to_all.24), kind=kLoop, calls=%fused_computation.24 | loop fusion | bytes 524288 | tf_op jit(solution)/shard_map/all_to_all | solution.py:205
  (13 shorter events, 0.2 us)
Async XLA Ops:
  0.0 13.3 %copy-start = (s32[8]{0:T(128)S(1)}, s32[8]{0:T(128)}, u32[]{:S(2)}) copy-start(s32[8]{0:T(128)} %param.9) | copy-start | bytes 100
  5.0 7.4 %copy-start.3 = (s32[8,4]{0,1:T(4,128)S(1)}, s32[8,4]{0,1:T(4,128)}, u32[]{:S(2)}) copy-start(s32[8,4]{0,1:T(4,128)} %param.10) | copy-start | bytes 388
  5.0 33.5 %all-to-all-start = ((bf16[8,130,4,128]{3,2,1,0:T(4,128)(2,1)}), bf16[8,130,4,128]{3,2,1,0:T(4,128)(2,1)S(1)}, u32[]{:S(2)}, u32[]{:S(2)}) async-start(bf16[8,130,4,128]{3,2,1,0:T(4,128)(2,1)} %copy.33), calls=%async_computation | async-start | bytes 2129920 | tf_op jit(solution)/shard_map/all_to_all | solution.py:13
  39.6 1.7 %copy-start.1 = (bf16[1025,32,32]{0,2,1:T(8,128)(2,1)S(1)}, bf16[1025,32,32]{0,2,1:T(8,128)(2,1)}, u32[]{:S(2)}) copy-start(bf16[1025,32,32]{0,2,1:T(8,128)(2,1)} %get-tuple-element.7) | copy-start | bytes 6297604
  39.7 2.4 %copy-start.2 = (bf16[1025,32,32]{0,2,1:T(8,128)(2,1)S(1)}, bf16[1025,32,32]{0,2,1:T(8,128)(2,1)}, u32[]{:S(2)}) copy-start(bf16[1025,32,32]{0,2,1:T(8,128)(2,1)} %get-tuple-element.8) | copy-start | bytes 6297604
